TPU v7x, 128 devices: a whole 4x4x4 slice. The times are simulated.
128 devices in a mesh: blk: 32 (over z, y, core), tp: 4 (over x).
Axes of the slice: x: 4, y: 4, z: 4, core: 2. Of those that a mesh axis runs over, the one named last changes fastest.
Arguments:
- tokens: bfloat16 [16384, 1664], P('blk', 'tp'), may hold values from -8 to 8
- block_split: int32 [64], replicated, may hold values from 0 to 63, each once
- req_lengths: int32 [128], replicated, may hold values from 1 to 125, as said below
- req_owners: int32 [128], replicated, may hold values from 0 to 31, as said below
- norm1_gain: float32 [1664], replicated, may hold values from 0.25 to 1.75
- qkv_weight: bfloat16 [1664, 3, 1664], P(None, None, 'tp'), may hold values from -2 to 2
- out_weight: bfloat16 [1664, 1664], P('tp'), may hold values from -0.15625 to 0.15625
- norm2_gain: float32 [1664], replicated, may hold values from 0.25 to 1.75
- up_weight: bfloat16 [1664, 8192], P(None, 'tp'), may hold values from -0.15625 to 0.15625
- down_weight: bfloat16 [8192, 1664], P('tp'), may hold values from -0.0625 to 0.0625
- merge_gain: float32 [1664], replicated, may hold values from 0.25 to 1.75
- merge_weight: bfloat16 [6656, 1664], P(None, 'tp'), may hold values from -0.078125 to 0.078125
Outputs:
- returned: bfloat16 [4096, 1664], P('blk', 'tp')
Inputs may be any that keep to these rules, and one draw needn't show every extreme that they name: Index d of blk holds packed blocks block_split[2d] and block_split[2d + 1], each of 256 tokens; every block once. `req_lengths`: lengths count merge groups of 4 tokens; the requests of each owner add up to exactly 128 groups. `req_owners`: every owner index holds exactly 4 requests.
All inputs are finite; a program needn't handle non-finite values.
Results may differ from a plain program's by a relative error of at most 0.015.
Values may be sent and summed in bfloat16 or wider, within the bound.
No kernel may reach another device: no remote copies, remote signals or barrier semaphores. Data moves between devices by JAX's collectives and lax.ppermute only.
A program may use at most 128 MiB of HBM per device.

v0:
```python
import math

import jax
import jax.numpy as jnp
from jax import lax
from jax.sharding import PartitionSpec as P

HDIM = 104


EPSILON = 1e-06
MASKED = -1e30


def layer_norm(values, norm_gain):
    values = values.astype(jnp.float32)
    row_mean = jnp.mean(values, axis=-1, keepdims=True)
    centred = values - row_mean
    spread = jnp.mean(centred * centred, axis=-1, keepdims=True)
    return centred * lax.rsqrt(spread + EPSILON) * norm_gain


def request_tables(req_lengths, req_owners):
    request_ends = jnp.cumsum(req_lengths)
    starts = request_ends - req_lengths
    position = jnp.arange(req_lengths.shape[0], dtype=jnp.int32)
    earlier = (req_owners[None, :] == req_owners[:, None]) & (position[None, :] < position[:, None])
    owner_offset = jnp.sum(jnp.where(earlier, req_lengths[None, :], 0), axis=1)
    return (starts, request_ends, owner_offset)


def segment_of(row_ids, block_split, request_ends, half_rows):
    slot_index = row_ids // half_rows
    places = jnp.arange(block_split.shape[0], dtype=jnp.int32)
    packed_block = jnp.sum(
        jnp.where(slot_index[:, None] == places[None, :], block_split[None, :], 0), axis=1
    )
    group_index = (packed_block * half_rows + row_ids % half_rows) // 4
    return jnp.sum((request_ends[None, :] <= group_index[:, None]).astype(jnp.int32), axis=1)


def owner_groups(
    owner, req_lengths, req_owners, block_split, starts, owner_offset, slot_count, half_groups
):
    slots = jnp.arange(slot_count, dtype=jnp.int32)
    chosen = (
        (req_owners[None, :] == owner)
        & (owner_offset[None, :] <= slots[:, None])
        & (slots[:, None] < (owner_offset + req_lengths)[None, :])
    )
    packed = jnp.sum(jnp.where(chosen, (starts - owner_offset)[None, :], 0), axis=1) + slots
    request = jnp.sum(
        jnp.where(chosen, jnp.arange(req_lengths.shape[0], dtype=jnp.int32)[None, :], 0), axis=1
    )
    packed_block = packed // half_groups
    places = jnp.arange(block_split.shape[0], dtype=jnp.int32)
    held_at = jnp.sum(
        jnp.where(block_split[None, :] == packed_block[:, None], places[None, :], 0), axis=1
    )
    return (held_at * half_groups + packed % half_groups, request)


def attend(carried, query_rows, query_seg, key_rows, value_rows, key_seg):
    maxima, totals, accumulated = carried
    query_count = query_rows.shape[0]
    key_count = key_rows.shape[0]
    head_count = accumulated.shape[1]
    head_size = accumulated.shape[2]
    query_heads = query_rows.reshape(query_count, head_count, head_size)
    key_heads = key_rows.reshape(key_count, head_count, head_size)
    value_heads = value_rows.reshape(key_count, head_count, head_size)
    scores = jnp.einsum(
        "qhd,khd->hqk", query_heads, key_heads, preferred_element_type=jnp.float32
    ) * head_size ** (-0.5)
    same_request = (query_seg[:, None] == key_seg[None, :])[None, :, :]
    scores = jnp.where(same_request, scores, MASKED)
    new_max = jnp.maximum(maxima, jnp.max(scores, axis=2))
    weights = jnp.where(same_request, jnp.exp(scores - new_max[:, :, None]), 0.0)
    factor = jnp.exp(maxima - new_max)
    totals = totals * factor + jnp.sum(weights, axis=2)
    mixed_values = jnp.einsum(
        "hqk,khd->qhd",
        weights.astype(jnp.bfloat16),
        value_heads,
        preferred_element_type=jnp.float32,
    )
    accumulated = accumulated * jnp.transpose(factor)[:, :, None] + mixed_values
    return (new_max, totals, accumulated)


def pick_rows(targets, carried, received):
    inside = (targets >= 0) & (targets < received.shape[0])
    picked = jnp.take(received, jnp.clip(targets, 0, received.shape[0] - 1), axis=0)
    return jnp.where(inside[:, None], picked, carried)


def body(
    tokens,
    block_split,
    req_lengths,
    req_owners,
    norm1_gain,
    qkv_weight,
    out_weight,
    norm2_gain,
    up_weight,
    down_weight,
    merge_gain,
    merge_weight,
):
    tok_rows = tokens.shape[0]
    half_rows = tok_rows // 2
    group_rows = tok_rows // 4
    my_index = lax.axis_index("blk")
    starts, request_ends, owner_offset = request_tables(req_lengths, req_owners)
    merged_targets, request = owner_groups(
        my_index,
        req_lengths,
        req_owners,
        block_split,
        starts,
        owner_offset,
        group_rows,
        half_rows // 4,
    )
    query_seg = segment_of(
        my_index * tok_rows + jnp.arange(tok_rows, dtype=jnp.int32),
        block_split,
        request_ends,
        half_rows,
    )
    features = lax.all_gather(tokens, "tp", axis=1, tiled=True)
    normed1 = layer_norm(features, norm1_gain).astype(jnp.bfloat16)
    projected = jnp.einsum(
        "td,dcf->ctf", normed1, qkv_weight, preferred_element_type=jnp.float32
    ).astype(jnp.bfloat16)
    queries = projected[0]
    head_count = qkv_weight.shape[2] // HDIM
    start_state = (
        jnp.full((head_count, tok_rows), MASKED, jnp.float32),
        jnp.zeros((head_count, tok_rows), jnp.float32),
        jnp.zeros((tok_rows, head_count, HDIM), jnp.float32),
    )
    carried = start_state
    key_piece = lax.all_gather(projected[1], "blk", axis=0, tiled=True)
    value_piece = lax.all_gather(projected[2], "blk", axis=0, tiled=True)
    key_count = key_piece.shape[0]
    block_rows = math.gcd(key_count, tok_rows * max(1, 1024 // tok_rows))
    key_seg = segment_of(
        jnp.arange(key_count, dtype=jnp.int32), block_split, request_ends, half_rows
    )
    stacked = (
        key_piece.reshape(key_count // block_rows, block_rows, -1),
        value_piece.reshape(key_count // block_rows, block_rows, -1),
        key_seg.reshape(key_count // block_rows, block_rows),
    )

    def visit_block(running, block_item):
        key_rows, value_rows, seg_rows = block_item
        touches = jnp.any(query_seg[:, None] == seg_rows[None, :])
        running = lax.cond(
            touches,
            lambda kept: attend(kept, queries, query_seg, key_rows, value_rows, seg_rows),
            lambda kept: kept,
            running,
        )
        return (running, None)

    carried, unused = lax.scan(visit_block, carried, stacked)
    running = carried
    maxima, totals, accumulated = running
    attended = (
        (accumulated / jnp.transpose(totals)[:, :, None]).reshape(tok_rows, -1).astype(jnp.bfloat16)
    )
    residual = features.astype(jnp.float32)
    after_attention = residual + lax.psum(
        jnp.dot(attended, out_weight, preferred_element_type=jnp.float32).astype(jnp.bfloat16), "tp"
    ).astype(jnp.float32)
    normed2 = layer_norm(after_attention, norm2_gain).astype(jnp.bfloat16)
    hidden = jax.nn.gelu(
        jnp.dot(normed2, up_weight, preferred_element_type=jnp.float32), approximate=False
    ).astype(jnp.bfloat16)
    after_mlp = after_attention + lax.psum(
        jnp.dot(hidden, down_weight, preferred_element_type=jnp.float32).astype(jnp.bfloat16), "tp"
    ).astype(jnp.float32)
    final_norm = layer_norm(after_mlp, merge_gain).astype(jnp.bfloat16)
    grouped = final_norm.reshape(group_rows, 4 * final_norm.shape[1])
    merged = jnp.dot(grouped, merge_weight, preferred_element_type=jnp.float32).astype(jnp.bfloat16)
    return pick_rows(
        merged_targets, jnp.zeros_like(merged), lax.all_gather(merged, "blk", axis=0, tiled=True)
    )


def solution(mesh):
    return jax.shard_map(
        body,
        mesh=mesh,
        in_specs=(
            P("blk", "tp"),
            P(),
            P(),
            P(),
            P(),
            P(None, None, "tp"),
            P("tp", None),
            P(),
            P(None, "tp"),
            P("tp", None),
            P(),
            P(None, "tp"),
        ),
        out_specs=P("blk", "tp"),
        check_vma=False,
    )
```

profile of v0, /device:TPU:1, one launch (start us, length us, event | category | flops | bytes accessed | tf_op | source)
XLA Modules:
  0.0 527.1 jit_solution(10143470909973689916)
XLA Ops:
  7.3 32.3 %all-gather.7.cloned.1.call-done = bf16[512,1664]{0,1:T(8,128)(2,1)} async-done(((bf16[512,416]{0,1:T(8,128)(2,1)}), bf16[512,1664]{0,1:T(8,128)(2,1)}) %all-gather.7.cloned.1.call-update) | async-done | bytes 1703952 | tf_op jit(solution)/shard_map/all_gather | solution.py:132
  39.6 2.7 copy.36
  43.3 4.9 fusion.79
  48.2 1.0 fusion.137
  51.0 1.6 reduce-window.8
  54.4 5.7 %convert_reduce_fusion = s32[16384]{0:T(1024)} fusion(s32[128]{0:T(128)S(1)} %reduce, s32[16384]{0:T(1024)S(1)} %add_select_fusion), kind=kLoop, calls=%fused_computation.21 | loop fusion | flops 6275072 | bytes 131584 | tf_op jit(solution)/shard_map/reduce_sum | solution.py:39
  60.1 1.5 reshape.327
  61.9 60.0 %all-gather.11.cloned.1.call-done = bf16[1,16384,416]{1,2,0:T(8,128)(2,1)} async-done(((bf16[1,512,416]{1,2,0:T(8,128)(2,1)}), bf16[1,16384,416]{1,2,0:T(8,128)(2,1)}) %all-gather.11.cloned.1.call-update) | async-done | bytes 13631504 | tf_op jit(solution)/shard_map/all_gather | solution.py:145
  122.0 13.8 %copy.42 = bf16[52,8,16,1024]{3,2,1,0:T(8,128)(2,1)S(1)} copy(bf16[52,8,16,1024]{3,1,2,0:T(8,128)(2,1)} %bitcast.76) | data formatting | bytes 27262976
  135.8 9.3 %copy.37 = bf16[16,1024,416]{1,2,0:T(8,128)(2,1)} copy(bf16[16,1024,416]{1,0,2:T(8,128)(2,1)S(1)} %bitcast.72) | data formatting | bytes 27262976 | tf_op jit(solution)/shard_map/while | solution.py:169
  145.1 51.0 %all-gather.13.cloned.1.call-done = bf16[1,16384,416]{1,2,0:T(8,128)(2,1)} async-done(((bf16[1,512,416]{1,2,0:T(8,128)(2,1)}), bf16[1,16384,416]{1,2,0:T(8,128)(2,1)}) %all-gather.13.cloned.1.call-update) | async-done | bytes 13631504 | tf_op jit(solution)/shard_map/all_gather | solution.py:146
  196.1 13.8 %copy.43 = bf16[52,8,16,1024]{3,2,1,0:T(8,128)(2,1)S(1)} copy(bf16[52,8,16,1024]{3,1,2,0:T(8,128)(2,1)} %bitcast.77) | data formatting | bytes 27262976
  209.9 9.3 %copy.38 = bf16[16,1024,416]{1,2,0:T(8,128)(2,1)} copy(bf16[16,1024,416]{1,0,2:T(8,128)(2,1)S(1)} %bitcast.73) | data formatting | bytes 27262976 | tf_op jit(solution)/shard_map/while | solution.py:169
  219.2 1.0 broadcast_in_dim.160
  220.2 77.3 %while.14 = (s32[]{:T(128)}, f32[4,512]{1,0:T(4,128)S(1)}, f32[4,512]{1,0:T(4,128)S(1)}, f32[512,4,104]{0,2,1:T(8,128)}, s32[512]{0:T(512)S(1)}, /*index=5*/s32[...) while((s32[]{:T(128)}, f32[4,512]{1,0:T(4,128)S(1)}, ...), condition=%wide.region_16.17_spmd, body=%wide.region_10.16_spmd.sunk | while | flops 901683200 | bytes 41472296 | solution.py:169
  221.5 1.0 compare_reduce_fusion.2
  223.1 9.4 %conditional.2 = ((f32[4,512]{1,0:T(4,128)S(1)}, f32[4,512]{1,0:T(4,128)S(1)}, f32[512,4,104]{0,2,1:T(8,128)})) conditional(s32[]{:T(128)} %convert_element_type.172, (f32[4,512]{1,0:T(4,128)S(1)}, f32[4,512]{1,0:T(4,128)S(1)}, f32[512,4,104]{0,2,1:T(8,128)}) %tuple.42, (s32[512]{0:T(512)S(1)}, s32[1024]{0:T(1024)S(1)}, ...), branch_computations={%region_12.12_spmd, %region_13.15_spmd} | conditional | flops 900634624 | bytes 41457756 | solution.py:161
  223.5 1.6 constant_dynamic-slice_fusion
  225.1 1.8 fusion
  226.9 2.1 fusion.2
  229.1 2.5 fusion.9
  233.3 1.0 compare_reduce_fusion.2
  235.8 1.0 compare_reduce_fusion.2
  237.4 9.4 %conditional.2 = ((f32[4,512]{1,0:T(4,128)S(1)}, f32[4,512]{1,0:T(4,128)S(1)}, f32[512,4,104]{0,2,1:T(8,128)})) conditional(s32[]{:T(128)} %convert_element_type.172, (f32[4,512]{1,0:T(4,128)S(1)}, f32[4,512]{1,0:T(4,128)S(1)}, f32[512,4,104]{0,2,1:T(8,128)}) %tuple.42, (s32[512]{0:T(512)S(1)}, s32[1024]{0:T(1024)S(1)}, ...), branch_computations={%region_12.12_spmd, %region_13.15_spmd} | conditional | flops 900634624 | bytes 41457756 | solution.py:161
  237.8 1.6 constant_dynamic-slice_fusion
  239.4 1.8 fusion
  241.2 2.1 fusion.2
  243.4 2.5 fusion.9
  247.6 1.0 compare_reduce_fusion.2
  250.0 1.0 compare_reduce_fusion.2
  251.7 9.4 %conditional.2 = ((f32[4,512]{1,0:T(4,128)S(1)}, f32[4,512]{1,0:T(4,128)S(1)}, f32[512,4,104]{0,2,1:T(8,128)})) conditional(s32[]{:T(128)} %convert_element_type.172, (f32[4,512]{1,0:T(4,128)S(1)}, f32[4,512]{1,0:T(4,128)S(1)}, f32[512,4,104]{0,2,1:T(8,128)}) %tuple.42, (s32[512]{0:T(512)S(1)}, s32[1024]{0:T(1024)S(1)}, ...), branch_computations={%region_12.12_spmd, %region_13.15_spmd} | conditional | flops 900634624 | bytes 41457756 | solution.py:161
  252.1 1.6 constant_dynamic-slice_fusion
  253.6 1.8 fusion
  255.5 2.1 fusion.2
  257.6 2.5 fusion.9
  261.8 1.0 compare_reduce_fusion.2
  264.3 1.0 compare_reduce_fusion.2
  266.8 1.0 compare_reduce_fusion.2
  269.2 1.0 compare_reduce_fusion.2
  271.7 1.0 compare_reduce_fusion.2
  274.2 1.0 compare_reduce_fusion.2
  276.6 1.0 compare_reduce_fusion.2
  278.3 9.4 %conditional.2 = ((f32[4,512]{1,0:T(4,128)S(1)}, f32[4,512]{1,0:T(4,128)S(1)}, f32[512,4,104]{0,2,1:T(8,128)})) conditional(s32[]{:T(128)} %convert_element_type.172, (f32[4,512]{1,0:T(4,128)S(1)}, f32[4,512]{1,0:T(4,128)S(1)}, f32[512,4,104]{0,2,1:T(8,128)}) %tuple.42, (s32[512]{0:T(512)S(1)}, s32[1024]{0:T(1024)S(1)}, ...), branch_computations={%region_12.12_spmd, %region_13.15_spmd} | conditional | flops 900634624 | bytes 41457756 | solution.py:161
  278.7 1.6 constant_dynamic-slice_fusion
  280.2 1.8 fusion
  282.1 2.1 fusion.2
  284.2 2.5 fusion.9
  288.4 1.0 compare_reduce_fusion.2
  290.9 1.0 compare_reduce_fusion.2
  293.4 1.0 compare_reduce_fusion.2
  295.8 1.0 compare_reduce_fusion.2
  297.5 1.3 divide_convert_fusion
  298.8 2.3 convolution_convert_fusion
  301.4 69.7 %all-reduce.3.cloned.1.call-done = bf16[512,1664]{1,0:T(8,128)(2,1)} async-done(((bf16[512,1664]{1,0:T(8,128)(2,1)}), bf16[512,1664]{1,0:T(8,128)(2,1)}) %all-reduce.3.cloned.1.call-update) | async-done | bytes 1703952 | tf_op jit(solution)/shard_map/psum | solution.py:176
  371.0 2.1 fusion.31
  374.0 21.8 %convolution_convert_fusion.1 = bf16[512,1664]{1,0:T(8,128)(2,1)} fusion(bf16[2048,1664]{1,0:T(8,128)(2,1)} %param.25, bf16[1664,2048]{1,0:T(8,128)(2,1)} %param.24, bf16[512,1664]{1,0:T(8,128)(2,1)} %all-reduce.3.cloned.1.call-done, bf16[512,1664]{1,0:T(8,128)(2,1)S(1)} %copy.36, f32[1664]{0:T(1024)S(1)} %copy-done.11, f32[512]{0:T(512)S(1)} %add_rsqrt_fusion.1, ...), kind=kOutput, calls=%fused_computation.57 | convolution fusion | flops 7054295040 | bytes 18754048 | tf_op jit(solution)/shard_map/dot_general | solution.py:184
  395.8 52.1 %all-reduce.5.cloned.1.call-done = bf16[512,1664]{1,0:T(8,128)(2,1)} async-done(((bf16[512,1664]{1,0:T(8,128)(2,1)}), bf16[512,1664]{1,0:T(8,128)(2,1)}) %all-reduce.5.cloned.1.call-update) | async-done | bytes 1703952 | tf_op jit(solution)/shard_map/psum | solution.py:183
  447.9 2.9 fusion.82
  451.9 2.1 multiply_convert_fusion
  454.0 3.0 reshape.330
  457.0 4.8 convolution_convert_fusion.2
  462.3 47.2 %all-gather.9.cloned.1.call-done = bf16[4096,416]{0,1:T(8,128)(2,1)} async-done(((bf16[128,416]{0,1:T(8,128)(2,1)}), bf16[4096,416]{0,1:T(8,128)(2,1)}) %all-gather.9.cloned.1.call-update) | async-done | bytes 3407888 | tf_op jit(solution)/shard_map/all_gather | solution.py:190
  509.5 6.1 %copy.39 = bf16[4096,416]{1,0:T(8,128)(2,1)} copy(bf16[4096,416]{0,1:T(8,128)(2,1)} %all-gather.9.cloned.1.call-done) | data formatting | bytes 6815744 | tf_op jit(solution)/shard_map/all_gather | solution.py:190
  515.6 3.6 gather_fusion
  (125 shorter events, 26.6 us)
Async XLA Ops:
  6.5 292.2 %copy-start = (bf16[416,1664]{1,0:T(8,128)(2,1)S(1)}, bf16[416,1664]{1,0:T(8,128)(2,1)}, u32[]{:S(2)}) copy-start(bf16[416,1664]{1,0:T(8,128)(2,1)} %param.22) | copy-start | bytes 4153348
  6.5 36.7 %copy-start.10 = (f32[1664]{0:T(1024)S(1)}, f32[1664]{0:T(1024)}, u32[]{:S(2)}) copy-start(f32[1664]{0:T(1024)} %param.20) | copy-start | bytes 19972
  6.5 33.0 %all-gather.7.cloned.1.call-start = ((), (), s32[]{:S(2)}) async-start(), calls=%async_computation | async-start | bytes 2129920 | tf_op jit(solution)/shard_map/all_gather | solution.py:132
  7.3 114.7 %all-gather.11.cloned.1.call-start = ((), (), s32[]{:S(2)}) async-start(), calls=%async_computation.4 | async-start | bytes 14057472 | tf_op jit(solution)/shard_map/all_gather | solution.py:145
  43.2 7.0 %copy-start.7 = (s32[128]{0:T(128)S(1)}, s32[128]{0:T(128)}, u32[]{:S(2)}) copy-start(s32[128]{0:T(128)} %param.18) | copy-start | bytes 1540
  43.2 10.3 %copy-start.8 = (s32[64]{0:T(128)S(1)}, s32[64]{0:T(128)}, u32[]{:S(2)}) copy-start(s32[64]{0:T(128)} %param.17) | copy-start | bytes 772
  49.2 146.9 %all-gather.13.cloned.1.call-start = ((), (), s32[]{:S(2)}) async-start(), calls=%async_computation.5 | async-start | bytes 14057472 | tf_op jit(solution)/shard_map/all_gather | solution.py:146
  49.9 321.1 %all-reduce.3.cloned.1.call-start = ((), (), s32[]{:S(2)}) async-start(), calls=%async_computation.1 | async-start | bytes 3407872 | tf_op jit(solution)/shard_map/psum | solution.py:176
  226.9 2.1 copy-start.4
  231.6 0.9 copy-start.5
  241.2 2.1 copy-start.4
  245.9 0.9 copy-start.5
  255.5 2.1 copy-start.4
  260.2 0.9 copy-start.5
  282.1 2.1 copy-start.4
  286.8 0.9 copy-start.5
  301.1 72.8 %copy-start.11 = (f32[1664]{0:T(1024)S(1)}, f32[1664]{0:T(1024)}, u32[]{:S(2)}) copy-start(f32[1664]{0:T(1024)} %param.23) | copy-start | bytes 19972
  301.1 146.8 %all-reduce.5.cloned.1.call-start = ((), (), s32[]{:S(2)}) async-start(), calls=%async_computation.2 | async-start | bytes 3407872 | tf_op jit(solution)/shard_map/psum | solution.py:183
  371.0 2.1 copy-start.1
  395.8 56.1 %copy-start.6 = (f32[1664]{0:T(1024)S(1)}, f32[1664]{0:T(1024)}, u32[]{:S(2)}) copy-start(f32[1664]{0:T(1024)} %param.26) | copy-start | bytes 19972
  395.8 113.8 %all-gather.9.cloned.1.call-start = ((), (), s32[]{:S(2)}) async-start(), calls=%async_computation.3 | async-start | bytes 3514368 | tf_op jit(solution)/shard_map/all_gather | solution.py:190
  447.9 2.9 copy-start.2
  447.9 3.0 copy-start.3
  457.0 4.8 copy-start.9
Sparse Core Ops, SparseCore 0:
  9.0 30.5 all-gather.6
  49.3 72.6 all-gather.10
  124.1 71.8 all-gather.12
  301.2 69.7 all-reduce.2
  395.9 52.0 all-reduce.4
  462.0 47.5 all-gather.8
where the time goes:
time: 532 us; the launch traced here: 527 us
  waiting for transfers between devices  314 us (59%)
  local copies, waits for them, and re-layouts  88.7 us (17%)
  matrix products  51.3 us (10%)
  other arithmetic  47.1 us (9%)
  between operations  14 us (3%)
  loops' own time  11.7 us (2%)
    psum x1, waiting for transfers between devices, body(): lax.psum(jnp.dot(attended, out_weight, preferred_element_type=jnp.float32...  69.7 us
    all_gather x1, waiting for transfers between devices, body(): key_piece = lax.all_gather(projected[1], 'blk', axis=0, tiled=True)  60 us
    psum x1, waiting for transfers between devices, body(): lax.psum(jnp.dot(hidden, down_weight, preferred_element_type=jnp.float32)...  52.1 us
    all_gather x1, waiting for transfers between devices, body(): value_piece = lax.all_gather(projected[2], 'blk', axis=0, tiled=True)  51 us
    all_gather x1, waiting for transfers between devices, body(): lax.all_gather(merged, 'blk', axis=0, tiled=True)  47.2 us
    all_gather x1, waiting for transfers between devices, body(): features = lax.all_gather(tokens, 'tp', axis=1, tiled=True)  32.3 us
    unnamed x22, local copies, waits for them, and re-layouts  27.7 us
    dot_general x1, matrix products, body(): jnp.dot(hidden, down_weight, preferred_element_type=jnp.float32)  21.8 us
  transfers between devices with their start and end apart: 6, of which 6 were waited for; matrix products, arithmetic and copies ran while one was open for 7% of the time, Pallas kernels for 0%

commit v1 on v0

v1 whole, which is shorter than its diff:
```python
import jax
import jax.numpy as jnp
from jax import lax
from jax.sharding import PartitionSpec as P

HDIM = 104


EPSILON = 1e-06
MASKED = -1e30


def layer_norm(values, norm_gain):
    values = values.astype(jnp.float32)
    row_mean = jnp.mean(values, axis=-1, keepdims=True)
    centred = values - row_mean
    spread = jnp.mean(centred * centred, axis=-1, keepdims=True)
    return centred * lax.rsqrt(spread + EPSILON) * norm_gain


def segment_at(positions, request_ends):
    return jnp.sum((request_ends[None, :] <= (positions // 4)[:, None]).astype(jnp.int32), axis=1)


def make_body(n_blk):
    def body(
        tokens,
        block_split,
        req_lengths,
        req_owners,
        norm1_gain,
        qkv_weight,
        out_weight,
        norm2_gain,
        up_weight,
        down_weight,
        merge_gain,
        merge_weight,
    ):
        tok_rows, width = tokens.shape
        half_rows = tok_rows // 2
        piece = half_rows // n_blk
        n_slots = block_split.shape[0]
        my_index = lax.axis_index("blk")

        slots = jnp.arange(n_slots, dtype=jnp.int32)
        inverse = jnp.sum(
            jnp.where(block_split[None, :] == slots[:, None], slots[None, :], 0), axis=1
        )
        spread = tokens.reshape(2, n_blk, piece, width).transpose(1, 0, 2, 3)
        spread = lax.all_to_all(spread, "blk", 0, 0, tiled=True)
        spread = spread.reshape(n_slots, piece, width)
        routed = jnp.take(spread, inverse, axis=0).reshape(n_blk, 2, piece, width)
        routed = lax.all_to_all(routed, "blk", 0, 0, tiled=True)
        local = routed.transpose(1, 0, 2, 3).reshape(tok_rows, width)

        request_ends = jnp.cumsum(req_lengths).astype(jnp.int32)
        starts = request_ends - req_lengths
        row_base = my_index * tok_rows
        query_seg = segment_at(row_base + jnp.arange(tok_rows, dtype=jnp.int32), request_ends)
        key_pos = row_base - tok_rows + jnp.arange(3 * tok_rows, dtype=jnp.int32)
        key_valid = (key_pos >= 0) & (key_pos < n_blk * tok_rows)
        key_seg = jnp.where(key_valid, segment_at(key_pos, request_ends), -1)

        features = lax.all_gather(local, "tp", axis=1, tiled=True)
        normed1 = layer_norm(features, norm1_gain).astype(jnp.bfloat16)
        projected = jnp.einsum(
            "td,dcf->ctf", normed1, qkv_weight, preferred_element_type=jnp.float32
        ).astype(jnp.bfloat16)
        queries = projected[0]
        key_value = projected[1:]
        from_prev = lax.ppermute(key_value, "blk", [(i, i + 1) for i in range(n_blk - 1)])
        from_next = lax.ppermute(key_value, "blk", [(i + 1, i) for i in range(n_blk - 1)])
        window = jnp.concatenate([from_prev, key_value, from_next], axis=1)

        head_count = qkv_weight.shape[2] // HDIM
        query_heads = queries.reshape(tok_rows, head_count, HDIM)
        key_heads = window[0].reshape(3 * tok_rows, head_count, HDIM)
        value_heads = window[1].reshape(3 * tok_rows, head_count, HDIM)
        scores = jnp.einsum(
            "qhd,khd->hqk", query_heads, key_heads, preferred_element_type=jnp.float32
        ) * HDIM ** (-0.5)
        same_request = (query_seg[:, None] == key_seg[None, :])[None, :, :]
        scores = jnp.where(same_request, scores, MASKED)
        maxima = jnp.max(scores, axis=2)
        weights = jnp.where(same_request, jnp.exp(scores - maxima[:, :, None]), 0.0)
        totals = jnp.sum(weights, axis=2)
        mixed = jnp.einsum(
            "hqk,khd->qhd",
            weights.astype(jnp.bfloat16),
            value_heads,
            preferred_element_type=jnp.float32,
        )
        attended = (mixed / jnp.transpose(totals)[:, :, None]).reshape(tok_rows, -1).astype(
            jnp.bfloat16
        )

        residual = features.astype(jnp.float32)
        after_attention = residual + lax.psum(
            jnp.dot(attended, out_weight, preferred_element_type=jnp.float32).astype(jnp.bfloat16),
            "tp",
        ).astype(jnp.float32)
        normed2 = layer_norm(after_attention, norm2_gain).astype(jnp.bfloat16)
        hidden = jax.nn.gelu(
            jnp.dot(normed2, up_weight, preferred_element_type=jnp.float32), approximate=False
        ).astype(jnp.bfloat16)
        after_mlp = after_attention + lax.psum(
            jnp.dot(hidden, down_weight, preferred_element_type=jnp.float32).astype(jnp.bfloat16),
            "tp",
        ).astype(jnp.float32)
        final_norm = layer_norm(after_mlp, merge_gain).astype(jnp.bfloat16)
        group_rows = tok_rows // 4
        grouped = final_norm.reshape(group_rows, 4 * final_norm.shape[1])
        merged = jnp.dot(grouped, merge_weight, preferred_element_type=jnp.float32).astype(
            jnp.bfloat16
        )
        out_width = merged.shape[1]

        all_groups = jnp.arange(n_blk * group_rows, dtype=jnp.int32)
        request = jnp.sum((request_ends[None, :] <= all_groups[:, None]).astype(jnp.int32), axis=1)
        position = jnp.arange(req_lengths.shape[0], dtype=jnp.int32)
        earlier = (req_owners[None, :] == req_owners[:, None]) & (position[None, :] < position[:, None])
        owner_offset = jnp.sum(jnp.where(earlier, req_lengths[None, :], 0), axis=1)
        shift = req_owners * group_rows + owner_offset - starts
        target = jnp.take(shift, request) + all_groups
        dest = target // group_rows

        rounds = group_rows // n_blk
        spread_m = merged.reshape(rounds, n_blk, out_width).transpose(1, 0, 2)
        spread_m = lax.all_to_all(spread_m, "blk", 0, 0, tiled=True)
        spread_m = spread_m.reshape(n_blk * rounds, out_width)
        held_local = jnp.arange(n_blk * rounds, dtype=jnp.int32)
        held_group = (held_local // rounds) * group_rows + (held_local % rounds) * n_blk + my_index
        held_dest = jnp.take(dest, held_group)
        same_dest = held_dest[:, None] == held_dest[None, :]
        before = held_local[None, :] < held_local[:, None]
        held_rank = jnp.sum((same_dest & before).astype(jnp.int32), axis=1)
        capacity = 8
        dest_ids = jnp.arange(n_blk, dtype=jnp.int32)
        cells = jnp.arange(capacity, dtype=jnp.int32)
        hit = (held_dest[None, None, :] == dest_ids[:, None, None]) & (
            held_rank[None, None, :] == cells[None, :, None]
        )
        send_index = jnp.sum(jnp.where(hit, held_local[None, None, :], 0), axis=2)
        send = jnp.take(spread_m, send_index.reshape(-1), axis=0).reshape(n_blk, capacity, out_width)
        received = lax.all_to_all(send, "blk", 0, 0, tiled=True).reshape(n_blk * capacity, out_width)

        my_slots = my_index * group_rows + jnp.arange(group_rows, dtype=jnp.int32)
        source = jnp.sum(
            jnp.where(target[None, :] == my_slots[:, None], all_groups[None, :], 0), axis=1
        )
        source_dev = source % n_blk
        same_src = source_dev[:, None] == source_dev[None, :]
        earlier_src = source[None, :] < source[:, None]
        cell = jnp.sum((same_src & earlier_src).astype(jnp.int32), axis=1)
        return jnp.take(received, source_dev * capacity + cell, axis=0)

    return body


def solution(mesh):
    n_blk = mesh.shape["blk"]
    return jax.shard_map(
        make_body(n_blk),
        mesh=mesh,
        in_specs=(
            P("blk", "tp"),
            P(),
            P(),
            P(),
            P(),
            P(None, None, "tp"),
            P("tp", None),
            P(),
            P(None, "tp"),
            P("tp", None),
            P(),
            P(None, "tp"),
        ),
        out_specs=P("blk", "tp"),
        check_vma=False,
    )
```

time: 532 us -> 305 us (0.57)
  waiting for transfers between devices: 314 us -> 137 us
  local copies, waits for them, and re-layouts: 88.7 us -> 41.4 us
  other arithmetic: 47.1 us -> 16.6 us
  starting transfers between devices: 0.67 us -> 27.6 us
  blocking collectives: 0 us -> 15.1 us
  loops' own time: 11.7 us -> 0 us
    all_gather x4 -> x1, waiting for transfers between devices: 190 us -> 23.9 us  [body(): features = lax.all_gather(local, 'tp', axis=1, tiled=True)]
    psum x1, waiting for transfers between devices: 69.7 us -> 27.9 us  [body(): lax.psum(jnp.dot(attended, out_weight, preferred_element_type=jnp.float32...]
    all_to_all x0 -> x3, waiting for transfers between devices: none -> 27 us  [the longest x1 10.5 us: body(): spread = lax.all_to_all(spread, 'blk', 0, 0, tiled=True)]
    unnamed x22 -> x19, local copies, waits for them, and re-layouts: 27.7 us -> 1.42 us
    gather x1 -> x5, local copies, waits for them, and re-layouts: 3.6 us -> 28.7 us  [the longest x1 24.7 us: body(): target = jnp.take(shift, request) + all_groups]
    all_to_all x0 -> x3, starting transfers between devices: none -> 21.5 us  [the longest x1 9.72 us: body(): spread = lax.all_to_all(spread, 'blk', 0, 0, tiled=True)]
    while x2 -> x0, local copies, waits for them, and re-layouts: 18.6 us -> none  [body(): carried, unused = lax.scan(visit_block, carried, stacked)]
    dynamic_slice x20 -> x0, local copies, waits for them, and re-layouts: 18.5 us -> none  [body(): carried, unused = lax.scan(visit_block, carried, stacked)]
  transfers between devices with their start and end apart: 6 -> 8, of which waited for: 6 -> 8; matrix products, arithmetic and copies ran while one was open for 7% -> 11% of each run, Pallas kernels for 0% -> 0%
where the time goes in v1:
time: 305 us; the launch traced here: 300 us
  waiting for transfers between devices  137 us (45%)
  matrix products  48.3 us (16%)
  local copies, waits for them, and re-layouts  41.4 us (14%)
  starting transfers between devices  27.6 us (9%)
  other arithmetic  16.6 us (5%)
  blocking collectives  15.1 us (5%)
  between operations  14 us (5%)
    psum x1, waiting for transfers between devices, body(): lax.psum(jnp.dot(hidden, down_weight, preferred_element_type=jnp.float32)...  50.7 us
    psum x1, waiting for transfers between devices, body(): lax.psum(jnp.dot(attended, out_weight, preferred_element_type=jnp.float32...  27.9 us
    gather x1, local copies, waits for them, and re-layouts, body(): target = jnp.take(shift, request) + all_groups  24.7 us
    all_gather x1, waiting for transfers between devices, body(): features = lax.all_gather(local, 'tp', axis=1, tiled=True)  23.9 us
    dot_general x1, matrix products, body(): jnp.dot(hidden, down_weight, preferred_element_type=jnp.float32)  21.8 us
    all_to_all x1, blocking collectives, body(): routed = lax.all_to_all(routed, 'blk', 0, 0, tiled=True)  15.1 us
    all_to_all x1, waiting for transfers between devices, body(): spread = lax.all_to_all(spread, 'blk', 0, 0, tiled=True)  10.5 us
    sub x1, matrix products, body(): weights = jnp.where(same_request, jnp.exp(scores - maxima[:, :, None]), 0.0)  9.92 us
  transfers between devices with their start and end apart: 8, of which 8 were waited for; matrix products, arithmetic and copies ran while one was open for 11% of the time, Pallas kernels for 0%

profile of v1, /device:TPU:1, one launch (start us, length us, event | category | flops | bytes accessed | tf_op | source)
XLA Modules:
  0.0 299.7 jit_solution(800821728085251753)
XLA Ops:
  6.5 1.3 copy.41
  7.9 0.9 copy.42
  8.7 9.7 %all-to-all-start = ((bf16[32,2,8,416]{3,2,1,0:T(8,128)(2,1)}), bf16[32,2,8,416]{3,2,1,0:T(8,128)(2,1)S(1)}, u32[]{:S(2)}, u32[]{:S(2)}) async-start(bf16[32,2,8,416]{3,2,1,0:T(8,128)(2,1)} %copy.42), calls=%async_computation | async-start | bytes 1048576 | tf_op jit(solution)/shard_map/all_to_all | solution.py:51
  18.5 0.8 select_reduce_fusion.3
  19.3 0.1 reduce_sum.162
  19.4 10.5 %all-to-all-done = bf16[32,2,8,416]{3,2,1,0:T(8,128)(2,1)S(1)} async-done(((bf16[32,2,8,416]{3,2,1,0:T(8,128)(2,1)}), bf16[32,2,8,416]{3,2,1,0:T(8,128)(2,1)S(1)}, u32[]{:S(2)}, u32[]{:S(2)}) %all-to-all-start) | async-done | bytes 426016 | tf_op jit(solution)/shard_map/all_to_all | solution.py:51
  29.9 0.6 gather_fusion.2
  30.5 0.1 broadcast_select_fusion
  30.6 15.1 %all_to_all.20 = bf16[32,2,8,416]{3,2,1,0:T(8,128)(2,1)S(1)} all-to-all(bf16[32,2,8,416]{3,2,1,0:T(8,128)(2,1)S(1)} %broadcast_select_fusion), channel_id=1, replica_groups=mesh['blk'=32,'tp'=4] {'blk'}, dimensions={0} | all-to-all | bytes 851968 | tf_op jit(solution)/shard_map/all_to_all | solution.py:54
  45.7 0.9 copy.44
  46.7 0.0 all-reduce.3.cloned.1.call-start
  46.8 0.1 copy.40
  46.9 0.2 reduce-window.8
  47.1 0.1 reduce
  47.2 0.5 convert_reduce_fusion.2
  47.7 23.9 %all-gather.2.cloned.1.call-done = bf16[512,1664]{0,1:T(8,128)(2,1)} async-done(((bf16[512,416]{0,1:T(8,128)(2,1)}), bf16[512,1664]{0,1:T(8,128)(2,1)}) %all-gather.2.cloned.1.call-update) | async-done | bytes 1703952 | tf_op jit(solution)/shard_map/all_gather | solution.py:65
  71.7 2.7 copy.45
  74.4 0.3 convert_reduce_fusion
  74.7 0.6 fusion.19
  75.3 4.9 %fusion.70 = bf16[3,512,416]{1,2,0:T(8,128)(2,1)S(1)} fusion(bf16[1664,3,416]{0,2,1:T(8,128)(2,1)} %param.17, bf16[512,1664]{1,0:T(8,128)(2,1)S(1)} %copy.45, f32[1664]{0:T(1024)S(1)} %copy-done.7, f32[512]{0:T(512)S(1)} %add_rsqrt_fusion.2, f32[512]{0:T(512)S(1)} %broadcast_multiply_fusion.2), kind=kOutput, calls=%fused_computation.94 | convolution fusion | flops 2131410944 | bytes 7145984 | tf_op jit(solution)/shard_map/td,dcf->ctf/dot_general | solution.py:67
  80.2 0.1 slice.26
  80.3 2.8 collective-permute-start.1
  83.0 3.2 %collective-permute-start = (bf16[2,512,416]{1,2,0:T(8,128)(2,1)S(1)}, bf16[2,512,416]{1,2,0:T(8,128)(2,1)S(1)}, u32[]{:S(2)}, u32[]{:S(2)}) collective-permute-start(bf16[2,512,416]{1,2,0:T(8,128)(2,1)S(1)} %slice.26), channel_id=1, source_target_pairs={{0,4},{4,8},{8,12},{12,16},{16,20},{20,24},{24,28},{28,32},{32,36}... | collective-permute-start | bytes 2555912 | tf_op jit(solution)/shard_map/ppermute | solution.py:72
  86.2 0.2 convert_reduce_fusion.3
  86.5 0.6 convert_reduce_fusion.1
  87.1 1.5 broadcast_compare_fusion
  88.6 5.9 %collective-permute-done.1 = bf16[2,512,416]{1,2,0:T(8,128)(2,1)S(1)} collective-permute-done((bf16[2,512,416]{1,2,0:T(8,128)(2,1)S(1)}, bf16[2,512,416]{1,2,0:T(8,128)(2,1)S(1)}, u32[]{:S(2)}, u32[]{:S(2)}) %collective-permute-start.1) | collective-permute-done | bytes 852000 | tf_op jit(solution)/shard_map/ppermute | solution.py:73
  94.5 1.2 collective-permute-done
  95.7 0.2 pad_maximum_fusion
  95.8 1.7 fusion.146
  97.5 9.9 %fusion.147 = (f32[4,512]{1,0:T(4,128)S(1)}, bf16[4,512,1536]{2,1,0:T(8,128)(2,1)}) fusion(pred[512,1536]{1,0:T(8,128)(4,1)} %broadcast_compare_fusion, bf16[512,4,104]{0,2,1:T(8,128)(2,1)S(1)} %bitcast.75, bf16[1536,4,104]{0,2,1:T(8,128)(2,1)} %bitcast.73), kind=kOutput, calls=%fused_computation.238 | convolution fusion | flops 673187328 | bytes 8790016 | tf_op jit(solution)/shard_map/sub | solution.py:86
  107.5 5.2 %fusion.81 = bf16[512,4,104]{0,2,1:T(8,128)(2,1)S(1)} fusion(bf16[1536,4,104]{0,2,1:T(8,128)(2,1)} %bitcast.72, bf16[4,512,1536]{2,1,0:T(8,128)(2,1)} %get-tuple-element.10, f32[512,4]{0,1:T(4,128)S(1)} %bitcast.81), kind=kOutput, calls=%fused_computation.98 | convolution fusion | flops 654737408 | bytes 8003584 | tf_op jit(solution)/shard_map/hqk,khd->qhd/dot_general | solution.py:88
  112.7 2.3 convolution_convert_fusion
  115.1 0.2 select_reduce_fusion.2
  115.3 24.7 %gather_fusion = s32[4096]{0:T(1024)S(1)} fusion(s32[128]{0:T(128)S(1)} %subtract_subtract_fusion, s32[4096]{0:T(1024)S(1)} %broadcast_clamp_fusion), kind=kCustom, calls=%fused_computation | custom fusion | bytes 49152 | tf_op jit(solution)/shard_map/jit(_take)/gather | solution.py:125
  140.1 1.4 gather_fusion.1
  141.5 0.2 convert_reduce_fusion.4
  141.7 27.9 %all-reduce.3.cloned.1.call-done = bf16[512,1664]{1,0:T(8,128)(2,1)} async-done(((bf16[512,1664]{1,0:T(8,128)(2,1)}), bf16[512,1664]{1,0:T(8,128)(2,1)}) %all-reduce.3.cloned.1.call-update) | async-done | bytes 1703952 | tf_op jit(solution)/shard_map/psum | solution.py:99
  169.6 2.1 fusion.22
  171.7 0.8 multiply_reduce_fusion.1
  172.5 21.8 %convolution_convert_fusion.1 = bf16[512,1664]{1,0:T(8,128)(2,1)} fusion(bf16[2048,1664]{1,0:T(8,128)(2,1)} %param.21, bf16[1664,2048]{1,0:T(8,128)(2,1)} %param.20, bf16[512,1664]{1,0:T(8,128)(2,1)} %all-reduce.3.cloned.1.call-done, bf16[512,1664]{1,0:T(8,128)(2,1)S(1)} %copy.45, f32[1664]{0:T(1024)S(1)} %copy-done.8, f32[512]{0:T(512)S(1)} %add_rsqrt_fusion.1, ...), kind=kOutput, calls=%fused_computation.47 | convolution fusion | flops 7054295040 | bytes 18754048 | tf_op jit(solution)/shard_map/dot_general | solution.py:108
  194.3 0.6 select_reduce_fusion.1
  195.0 0.1 reshape.550
  195.1 0.4 select_reduce_fusion
  195.5 0.2 convert_reduce_fusion.5
  195.8 50.7 %all-reduce.5.cloned.1.call-done = bf16[512,1664]{1,0:T(8,128)(2,1)} async-done(((bf16[512,1664]{1,0:T(8,128)(2,1)}), bf16[512,1664]{1,0:T(8,128)(2,1)}) %all-reduce.5.cloned.1.call-update) | async-done | bytes 1703952 | tf_op jit(solution)/shard_map/psum | solution.py:107
  246.5 2.9 fusion.84
  249.4 0.1 copy-done.3
  249.5 1.0 multiply_reduce_fusion
  250.5 2.1 multiply_convert_fusion
  252.6 3.0 reshape.547
  255.6 4.2 %convolution_convert_fusion.2 = bf16[128,416]{0,1:T(8,128)(2,1)S(1)} fusion(bf16[128,6656]{1,0:T(8,128)(2,1)S(1)} %reshape.547, bf16[6656,416]{0,1:T(8,128)(2,1)} %param.23), kind=kOutput, calls=%fused_computation.99 | convolution fusion | flops 708890624 | bytes 7348224 | tf_op jit(solution)/shard_map/dot_general | solution.py:114
  259.7 0.1 copy.46
  259.9 0.7 copy.47
  260.6 7.9 %all-to-all-start.2 = ((bf16[32,4,416]{2,1,0:T(4,128)(2,1)}), bf16[32,4,416]{2,1,0:T(4,128)(2,1)S(1)}, u32[]{:S(2)}, u32[]{:S(2)}) async-start(bf16[32,4,416]{2,1,0:T(4,128)(2,1)} %copy.47), calls=%async_computation.2 | async-start | bytes 262144 | tf_op jit(solution)/shard_map/all_to_all | solution.py:130
  268.5 7.6 %all-to-all-done.2 = bf16[32,4,416]{2,1,0:T(4,128)(2,1)S(1)} async-done(((bf16[32,4,416]{2,1,0:T(4,128)(2,1)}), bf16[32,4,416]{2,1,0:T(4,128)(2,1)S(1)}, u32[]{:S(2)}, u32[]{:S(2)}) %all-to-all-start.2) | async-done | bytes 106528 | tf_op jit(solution)/shard_map/all_to_all | solution.py:130
  276.1 0.1 reshape.549
  276.1 1.2 gather_fusion.3
  277.3 0.8 bitcast_select_fusion
  278.1 3.9 %all-to-all-start.3 = ((bf16[32,8,416]{2,1,0:T(8,128)(2,1)}), bf16[32,8,416]{2,1,0:T(8,128)(2,1)S(1)}, u32[]{:S(2)}, u32[]{:S(2)}) async-start(bf16[32,8,416]{2,1,0:T(8,128)(2,1)} %bitcast_select_fusion), calls=%async_computation.3 | async-start | bytes 524288 | tf_op jit(solution)/shard_map/all_to_all | solution.py:146
  282.1 9.0 %all-to-all-done.3 = bf16[32,8,416]{2,1,0:T(8,128)(2,1)S(1)} async-done(((bf16[32,8,416]{2,1,0:T(8,128)(2,1)}), bf16[32,8,416]{2,1,0:T(8,128)(2,1)S(1)}, u32[]{:S(2)}, u32[]{:S(2)}) %all-to-all-start.3) | async-done | bytes 213024 | tf_op jit(solution)/shard_map/all_to_all | solution.py:146
  291.0 0.8 gather_fusion.4
  291.9 0.1 broadcast_select_fusion.1
  292.0 0.8 copy.48
  (53 shorter events, 0.5 us)
Async XLA Ops:
  6.5 106.2 %copy-start = (bf16[416,1664]{1,0:T(8,128)(2,1)S(1)}, bf16[416,1664]{1,0:T(8,128)(2,1)}, u32[]{:S(2)}) copy-start(bf16[416,1664]{1,0:T(8,128)(2,1)} %param.18) | copy-start | bytes 4153348
  8.7 38.0 %copy-start.5 = (s32[128]{0:T(128)S(1)}, s32[128]{0:T(128)}, u32[]{:S(2)}) copy-start(s32[128]{0:T(128)} %param.14) | copy-start | bytes 1540
  8.7 21.2 %all-to-all-start = ((bf16[32,2,8,416]{3,2,1,0:T(8,128)(2,1)}), bf16[32,2,8,416]{3,2,1,0:T(8,128)(2,1)S(1)}, u32[]{:S(2)}, u32[]{:S(2)}) async-start(bf16[32,2,8,416]{3,2,1,0:T(8,128)(2,1)} %copy.42), calls=%async_computation | async-start | bytes 1048576 | tf_op jit(solution)/shard_map/all_to_all | solution.py:51
  18.5 53.2 %all-gather.2.cloned.1.call-start = ((), (), s32[]{:S(2)}) async-start(), calls=%async_computation.4 | async-start | bytes 2129920 | tf_op jit(solution)/shard_map/all_gather | solution.py:65
  46.7 122.9 %all-reduce.3.cloned.1.call-start = ((), (), s32[]{:S(2)}) async-start(), calls=%async_computation.5 | async-start | bytes 3407872 | tf_op jit(solution)/shard_map/psum | solution.py:99
  47.7 27.6 %copy-start.7 = (f32[1664]{0:T(1024)S(1)}, f32[1664]{0:T(1024)}, u32[]{:S(2)}) copy-start(f32[1664]{0:T(1024)} %param.16) | copy-start | bytes 19972
  80.3 14.2 %collective-permute-start.1 = (bf16[2,512,416]{1,2,0:T(8,128)(2,1)S(1)}, bf16[2,512,416]{1,2,0:T(8,128)(2,1)S(1)}, u32[]{:S(2)}, u32[]{:S(2)}) collective-permute-start(bf16[2,512,416]{1,2,0:T(8,128)(2,1)S(1)} %slice.26), channel_id=1, source_target_pairs={{4,0},{8,4},{12,8},{16,12},{20,16},{24,20},{28,24},{32,28},{36,32}... | collective-permute-start | bytes 2555912 | tf_op jit(solution)/shard_map/ppermute | solution.py:73
  83.0 12.6 %collective-permute-start = (bf16[2,512,416]{1,2,0:T(8,128)(2,1)S(1)}, bf16[2,512,416]{1,2,0:T(8,128)(2,1)S(1)}, u32[]{:S(2)}, u32[]{:S(2)}) collective-permute-start(bf16[2,512,416]{1,2,0:T(8,128)(2,1)S(1)} %slice.26), channel_id=1, source_target_pairs={{0,4},{4,8},{8,12},{12,16},{16,20},{20,24},{24,28},{28,32},{32,36}... | collective-permute-start | bytes 2555912 | tf_op jit(solution)/shard_map/ppermute | solution.py:72
  112.7 2.4 copy-start.6
  115.1 131.4 %all-reduce.5.cloned.1.call-start = ((), (), s32[]{:S(2)}) async-start(), calls=%async_computation.6 | async-start | bytes 3407872 | tf_op jit(solution)/shard_map/psum | solution.py:107
  141.7 30.8 %copy-start.8 = (f32[1664]{0:T(1024)S(1)}, f32[1664]{0:T(1024)}, u32[]{:S(2)}) copy-start(f32[1664]{0:T(1024)} %param.19) | copy-start | bytes 19972
  169.6 2.1 copy-start.1
  246.5 2.9 copy-start.2
  246.5 3.0 copy-start.3
  249.4 1.1 copy-start.4
  260.6 15.5 %all-to-all-start.2 = ((bf16[32,4,416]{2,1,0:T(4,128)(2,1)}), bf16[32,4,416]{2,1,0:T(4,128)(2,1)S(1)}, u32[]{:S(2)}, u32[]{:S(2)}) async-start(bf16[32,4,416]{2,1,0:T(4,128)(2,1)} %copy.47), calls=%async_computation.2 | async-start | bytes 262144 | tf_op jit(solution)/shard_map/all_to_all | solution.py:130
  278.1 12.9 %all-to-all-start.3 = ((bf16[32,8,416]{2,1,0:T(8,128)(2,1)}), bf16[32,8,416]{2,1,0:T(8,128)(2,1)S(1)}, u32[]{:S(2)}, u32[]{:S(2)}) async-start(bf16[32,8,416]{2,1,0:T(8,128)(2,1)} %bitcast_select_fusion), calls=%async_computation.3 | async-start | bytes 524288 | tf_op jit(solution)/shard_map/all_to_all | solution.py:146
Sparse Core Ops, SparseCore 0:
  46.8 24.7 all-gather.1
  115.2 54.3 all-reduce.2
  194.5 51.9 all-reduce.4
